TPU v7x, 512 devices: a whole 4x8x8 slice. The times are simulated.
512 devices in a mesh: blk: 16 (over y_hi, z), bank: 32 (over y_lo, x, core).
Axes of the slice: x: 4, y: 8 (y_hi: 2, y_lo: 4; y = y_hi * 4 + y_lo), z: 8, core: 2. Of those that a mesh axis runs over, the one named last changes fastest.
Arguments:
- log_density: bfloat16 [2048, 32768], P(('blk', 'bank')), may hold values from -8 to 8
- assignment: int32 [2048], P(('blk', 'bank')), may hold values from 0 to 7, as said below
Outputs:
- centers: bfloat16 [8, 32768], P(None, 'bank')
- potentials: float32 [2048, 32768], P(('blk', 'bank'))
Inputs may be any that keep to these rules, and one draw needn't show every extreme that they name: Every barycenter index is the assignment of at least one member.
All inputs are finite; a program needn't handle non-finite values.
Results may differ from a plain program's by a relative error of at most 0.0051.
Values may be sent and summed in bfloat16 or wider, within the bound.
No kernel may reach another device: no remote copies, remote signals or barrier semaphores. Data moves between devices by JAX's collectives and lax.ppermute only.
A program may use at most 64 MiB of HBM per device.

v0:
```python
import jax
import jax.numpy as jnp
from jax import lax
from jax.sharding import PartitionSpec as P

G = 32
BARS = 8
ITERS = 2


def kernel_tables():
    grid_pos = jnp.arange(G, dtype=jnp.float32)
    offset = grid_pos[:, None] - grid_pos[None, :]
    kernel_line = jnp.exp(-0.5 * offset * offset)
    kernel_pair = (
        (kernel_line[:, None, :, None] * kernel_line[None, :, None, :])
        .reshape(G * G, G * G)
        .astype(jnp.bfloat16)
    )
    return (kernel_line, kernel_pair)


def log_convolve(field_log, kernel_line, kernel_pair):
    member_count = field_log.shape[0]
    raised = jnp.exp(field_log).astype(jnp.bfloat16).reshape(member_count * G, G * G)
    inner_sum = jnp.dot(raised, kernel_pair, preferred_element_type=jnp.float32).reshape(
        member_count, G, G * G
    )
    outer_sum = jnp.einsum("ij,mjc->mic", kernel_line, inner_sum, precision=lax.Precision.HIGHEST)
    return jnp.log(outer_sum).reshape(member_count, G * G * G)


def per_device(log_density, assignment):
    kernel_line, kernel_pair = kernel_tables()
    member_count = log_density.shape[0]
    cell_count = log_density.shape[1]
    row_count = cell_count // 128
    labels = jnp.arange(BARS, dtype=jnp.int32)
    onehot = (assignment[:, None] == labels[None, :]).astype(jnp.float32)
    counts = lax.psum(jnp.sum(onehot, axis=0), ("blk", "bank"))
    selector = onehot.astype(jnp.bfloat16)
    member_weights = jnp.transpose(onehot)
    potential = jnp.zeros((member_count, cell_count), jnp.float32)
    center_owned = jnp.zeros((row_count // lax.axis_size("bank"), BARS, 128), jnp.bfloat16)
    for iteration in range(ITERS):
        source = log_density.astype(jnp.float32) - log_convolve(potential, kernel_line, kernel_pair)
        smoothed = log_convolve(source, kernel_line, kernel_pair)
        blocks = smoothed.reshape(member_count, row_count, 128)
        reduced = lax.psum_scatter(
            jnp.einsum("km,mrl->rkl", member_weights, blocks, precision=lax.Precision.HIGHEST),
            "bank",
            scatter_dimension=0,
            tiled=True,
        )
        summed = lax.psum(reduced, "blk")
        center_slice = (summed / counts[None, :, None]).astype(jnp.bfloat16)
        center_all = lax.all_gather(center_slice, "bank", axis=0, tiled=True)
        center_owned = center_slice
        chosen = jnp.einsum("mk,rkl->mrl", selector, center_all, preferred_element_type=jnp.float32)
        potential = chosen.reshape(member_count, cell_count) - smoothed
    centers = jnp.transpose(center_owned, (1, 0, 2)).reshape(BARS, center_owned.shape[0] * 128)
    return (centers, potential)


def solution(mesh):
    placed = (P(("blk", "bank"), None), P(("blk", "bank")))
    return jax.shard_map(
        per_device,
        mesh=mesh,
        in_specs=placed,
        out_specs=(P(None, "bank"), P(("blk", "bank"), None)),
        check_vma=False,
    )
```

profile of v0, /device:TPU:1, one launch (start us, length us, event | category | flops | bytes accessed | tf_op | source)
XLA Modules:
  0.0 615.1 jit_solution(17114058292738188008)
XLA Ops:
  7.2 0.0 reduce-scatter.3.cloned.1.call-start
  7.2 5.3 multiply_convert_fusion
  12.5 11.3 %reshape.101 = bf16[1024,1024,1]{1,0,2:T(8,128)(2,1)S(1)} reshape(bf16[32,32,32,32]{3,2,1,0:T(8,128)(2,1)} %multiply_convert_fusion) | data formatting | bytes 4194304 | tf_op jit(solution)/shard_map/convert_element_type | solution.py:18
  23.8 0.0 copy-start
  23.8 0.4 fusion.17
  24.3 0.6 fusion.3
  24.9 0.3 copy.9
  25.2 0.0 copy-done
  25.2 0.2 fusion.5
  25.4 0.0 copy-start.1
  25.5 0.5 fusion.14
  25.9 0.6 fusion.2
  26.5 0.1 reshape_reshape.6
  26.6 0.0 copy-done.1
  26.6 2.0 convolution_bitcast_fusion.2
  28.6 0.0 reduce-scatter.3.cloned.1.call-update
  28.6 0.0 reduce-scatter.5.cloned.1.call-start
  28.7 0.1 convert_reduce_fusion
  28.8 108.1 %psum.22 = f32[8]{0:T(128)S(1)} all-reduce(f32[8]{0:T(128)S(1)} %convert_reduce_fusion), channel_id=1, replica_groups=mesh['blk'=16,'bank'=32] {'blk','bank'}, use_global_device_ids=true, to_apply=%region_3.0 | all-reduce | flops 8 | bytes 64 | tf_op jit(solution)/shard_map/psum | solution.py:40
  136.9 42.7 %reduce-scatter.3.cloned.1.call-done = f32[8,8,128]{2,1,0:T(8,128)} async-done(((f32[256,8,128]{2,1,0:T(8,128)}), f32[8,8,128]{2,1,0:T(8,128)}) %reduce-scatter.3.cloned.1.call-update) | async-done | bytes 32784 | tf_op jit(solution)/shard_map/reduce_scatter | solution.py:49
  179.6 85.1 %psum.21 = f32[8,8,128]{2,1,0:T(8,128)S(1)} all-reduce(f32[8,8,128]{2,1,0:T(8,128)} %reduce-scatter.3.cloned.1.call-done), channel_id=1, replica_groups=mesh['blk'=16,'bank'=32] {'blk'}, use_global_device_ids=true, to_apply=%region_1.0 | all-reduce | flops 8192 | bytes 65536 | tf_op jit(solution)/shard_map/psum | solution.py:55
  264.7 0.1 divide_convert_fusion.1
  264.7 55.8 %all_gather.6 = bf16[256,8,128]{2,1,0:T(8,128)(2,1)S(1)} all-gather(bf16[8,8,128]{2,1,0:T(8,128)(2,1)S(1)} %divide_convert_fusion.1), channel_id=1, replica_groups=mesh['blk'=16,'bank'=32] {'bank'}, dimensions={0}, use_global_device_ids=true | all-gather | bytes 540672 | tf_op jit(solution)/shard_map/all_gather | solution.py:57
  320.6 0.3 fusion.37
  320.9 0.8 copy.6
  321.7 1.1 reshape.96
  322.9 0.5 fusion.10
  323.3 0.6 fusion.1
  323.9 0.3 copy.11
  324.3 0.2 fusion.7
  324.5 0.5 fusion.11
  325.0 0.6 convolution_log_fusion
  325.6 0.1 reshape_reshape.7
  325.7 2.0 convolution_bitcast_fusion.1
  327.6 0.0 reduce-scatter.5.cloned.1.call-update
  327.6 0.3 copy.13
  328.0 137.6 %reduce-scatter.5.cloned.1.call-done = f32[8,8,128]{2,1,0:T(8,128)} async-done(((f32[256,8,128]{2,1,0:T(8,128)}), f32[8,8,128]{2,1,0:T(8,128)}) %reduce-scatter.5.cloned.1.call-update) | async-done | bytes 32784 | tf_op jit(solution)/shard_map/reduce_scatter | solution.py:49
  465.6 85.1 %psum.23 = f32[8,8,128]{2,1,0:T(8,128)S(1)} all-reduce(f32[8,8,128]{2,1,0:T(8,128)} %reduce-scatter.5.cloned.1.call-done), channel_id=1, replica_groups=mesh['blk'=16,'bank'=32] {'blk'}, use_global_device_ids=true, to_apply=%region_5.0 | all-reduce | flops 8192 | bytes 65536 | tf_op jit(solution)/shard_map/psum | solution.py:55
  550.7 0.1 divide_convert_fusion
  550.8 0.7 fusion.58
  551.5 55.6 %all_gather.7 = bf16[256,8,128]{2,1,0:T(8,128)(2,1)S(1)} all-gather(bf16[8,8,128]{2,1,0:T(8,128)(2,1)S(1)} %divide_convert_fusion), channel_id=1, replica_groups=mesh['blk'=16,'bank'=32] {'bank'}, dimensions={0}, use_global_device_ids=true | all-gather | bytes 540672 | tf_op jit(solution)/shard_map/all_gather | solution.py:57
  607.1 1.1 fusion
  (1 shorter events, 0.0 us)
Async XLA Ops:
  7.2 172.4 %reduce-scatter.3.cloned.1.call-start = ((), (), s32[]{:S(2)}) async-start(), calls=%async_computation.2 | async-start | bytes 1081344 | tf_op jit(solution)/shard_map/reduce_scatter | solution.py:49
  23.8 1.4 copy-start
  25.4 1.2 copy-start.1
  28.6 436.9 %reduce-scatter.5.cloned.1.call-start = ((), (), s32[]{:S(2)}) async-start(), calls=%async_computation.3 | async-start | bytes 1081344 | tf_op jit(solution)/shard_map/reduce_scatter | solution.py:49
Sparse Core Ops, SparseCore 0:
  28.7 150.7 reduce-scatter.2
  327.8 137.7 reduce-scatter.4
where the time goes:
time: 616 us; the launch traced here: 615 us
  blocking collectives  390 us (63%)
  waiting for transfers between devices  180 us (29%)
  local copies, waits for them, and re-layouts  14.5 us (2%)
  between operations  14.2 us (2%)
  matrix products  9.63 us (2%)
  other arithmetic  6.6 us (1%)
    reduce_scatter x2, waiting for transfers between devices, per_device(): lax.psum_scatter(jnp.einsum('km,mrl->rkl', member_weights, blocks, precis...  180 us
    psum x2, blocking collectives, per_device(): summed = lax.psum(reduced, 'blk')  170 us
    all_gather x2, blocking collectives, per_device(): center_all = lax.all_gather(center_slice, 'bank', axis=0, tiled=True)  111 us
    psum x1, blocking collectives, per_device(): counts = lax.psum(jnp.sum(onehot, axis=0), ('blk', 'bank'))  108 us
  transfers between devices with their start and end apart: 2, of which 2 were waited for; matrix products, arithmetic and copies ran while one was open for 0% of the time, Pallas kernels for 0%

commit v1 on v0

--- a/solution.py
+++ b/solution.py
@@ -54,7 +54,16 @@
         )
         summed = lax.psum(reduced, "blk")
         center_slice = (summed / counts[None, :, None]).astype(jnp.bfloat16)
-        center_all = lax.all_gather(center_slice, "bank", axis=0, tiled=True)
+        divide_indices = lambda panel: jnp.concatenate(
+            jax.lax.all_to_all(
+                jnp.stack([panel for _ in range(jax.lax.axis_size("bank"))], 0),
+                axis_name="bank",
+                split_axis=0,
+                concat_axis=0,
+            ),
+            0,
+        )
+        center_all = divide_indices(center_slice)
         center_owned = center_slice
         chosen = jnp.einsum("mk,rkl->mrl", selector, center_all, preferred_element_type=jnp.float32)
         potential = chosen.reshape(member_count, cell_count) - smoothed

time: 616 us -> 578 us (0.938)
  blocking collectives: 390 us -> 278 us
  starting transfers between devices: 0.08 us -> 42 us
  waiting for transfers between devices: 180 us -> 211 us
    all_gather x2 -> x0, blocking collectives: 111 us -> none  [per_device(): center_all = lax.all_gather(center_slice, 'bank', axis=0, tiled=True)]
    all_to_all x0 -> x2, starting transfers between devices: none -> 41.8 us  [per_device(): jax.lax.all_to_all(jnp.stack([panel for _ in range(jax.lax.axis_size('ban...]
    all_to_all x0 -> x2, waiting for transfers between devices: none -> 30.7 us  [per_device(): jax.lax.all_to_all(jnp.stack([panel for _ in range(jax.lax.axis_size('ban...]
  transfers between devices with their start and end apart: 2 -> 4, of which waited for: 2 -> 4; matrix products, arithmetic and copies ran while one was open for 0% -> 0% of each run, Pallas kernels for 0% -> 0%
where the time goes in v1:
time: 578 us
  blocking collectives  278 us (48%)
  waiting for transfers between devices  211 us (37%)
  starting transfers between devices  42 us (7%)
  local copies, waits for them, and re-layouts  15.5 us (3%)
  between operations  14.2 us (2%)
  matrix products  10.7 us (2%)
  other arithmetic  6.59 us (1%)
    reduce_scatter x2, waiting for transfers between devices, per_device(): lax.psum_scatter(jnp.einsum('km,mrl->rkl', member_weights, blocks, precis...  180 us
    psum x2, blocking collectives, per_device(): summed = lax.psum(reduced, 'blk')  170 us
    psum x1, blocking collectives, per_device(): counts = lax.psum(jnp.sum(onehot, axis=0), ('blk', 'bank'))  108 us
    all_to_all x2, starting transfers between devices, per_device(): jax.lax.all_to_all(jnp.stack([panel for _ in range(jax.lax.axis_size('ban...  41.8 us
    all_to_all x2, waiting for transfers between devices, per_device(): jax.lax.all_to_all(jnp.stack([panel for _ in range(jax.lax.axis_size('ban...  30.7 us
  transfers between devices with their start and end apart: 4, of which 4 were waited for; matrix products, arithmetic and copies ran while one was open for 0% of the time, Pallas kernels for 0%

profile of v1, /device:TPU:1, one launch (start us, length us, event | category | flops | bytes accessed | tf_op | source)
XLA Modules:
  0.0 577.6 jit_solution(9502267768342563470)
XLA Ops:
  7.2 0.0 reduce-scatter.3.cloned.1.call-start
  7.2 5.3 multiply_convert_fusion
  12.5 11.3 %reshape.114 = bf16[1024,1024,1]{1,0,2:T(8,128)(2,1)S(1)} reshape(bf16[32,32,32,32]{3,2,1,0:T(8,128)(2,1)} %multiply_convert_fusion) | data formatting | bytes 4194304 | tf_op jit(solution)/shard_map/convert_element_type | solution.py:18
  23.8 0.0 copy-start
  23.8 0.4 fusion.19
  24.3 0.6 fusion.3
  24.9 0.3 copy.8
  25.2 0.0 copy-done
  25.2 0.2 fusion.5
  25.4 0.0 copy-start.1
  25.5 0.5 fusion.16
  25.9 0.6 convolution_log_fusion.2
  26.5 0.1 reshape_reshape.6
  26.6 0.0 copy-done.1
  26.6 2.0 convolution_bitcast_fusion.1
  28.6 0.0 reduce-scatter.3.cloned.1.call-update
  28.6 0.1 convert_reduce_fusion
  28.7 108.2 %psum.22 = f32[8]{0:T(128)S(1)} all-reduce(f32[8]{0:T(128)S(1)} %convert_reduce_fusion), channel_id=1, replica_groups=mesh['blk'=16,'bank'=32] {'blk','bank'}, use_global_device_ids=true, to_apply=%region_3.0 | all-reduce | flops 8 | bytes 64 | tf_op jit(solution)/shard_map/psum | solution.py:40
  136.9 42.6 %reduce-scatter.3.cloned.1.call-done = f32[8,8,128]{2,1,0:T(8,128)} async-done(((f32[256,8,128]{2,1,0:T(8,128)}), f32[8,8,128]{2,1,0:T(8,128)}) %reduce-scatter.3.cloned.1.call-update) | async-done | bytes 32784 | tf_op jit(solution)/shard_map/reduce_scatter | solution.py:49
  179.5 84.6 %psum.21 = f32[8,8,128]{2,1,0:T(8,128)S(1)} all-reduce(f32[8,8,128]{2,1,0:T(8,128)} %reduce-scatter.3.cloned.1.call-done), channel_id=1, replica_groups=mesh['blk'=16,'bank'=32] {'blk'}, use_global_device_ids=true, to_apply=%region_1.0 | all-reduce | flops 8192 | bytes 65536 | tf_op jit(solution)/shard_map/psum | solution.py:55
  264.1 0.1 divide_convert_fusion.1
  264.2 0.9 stack.4
  265.1 21.0 %all-to-all-start = ((bf16[32,8,8,128]{3,2,1,0:T(8,128)(2,1)}), bf16[32,8,8,128]{3,2,1,0:T(8,128)(2,1)S(1)}, u32[]{:S(2)}, u32[]{:S(2)}) async-start(bf16[32,8,8,128]{3,2,1,0:T(8,128)(2,1)} %stack.4), calls=%async_computation.1 | async-start | bytes 1048576 | tf_op jit(solution)/shard_map/all_to_all | solution.py:58
  286.1 0.2 reduce-scatter.5.cloned.1.call-start
  286.4 1.1 copy.10
  287.5 15.2 %all-to-all-done = bf16[32,8,8,128]{3,2,1,0:T(8,128)(2,1)S(1)} async-done(((bf16[32,8,8,128]{3,2,1,0:T(8,128)(2,1)}), bf16[32,8,8,128]{3,2,1,0:T(8,128)(2,1)S(1)}, u32[]{:S(2)}, u32[]{:S(2)}) %all-to-all-start) | async-done | bytes 524320 | tf_op jit(solution)/shard_map/all_to_all | solution.py:58
  302.7 1.4 fusion.1
  304.1 0.5 fusion.13
  304.6 0.6 fusion.2
  305.2 0.3 copy.12
  305.5 0.2 fusion.7
  305.7 0.5 fusion.10
  306.2 0.6 convolution_log_fusion
  306.8 0.1 reshape_reshape.7
  306.9 2.0 convolution_bitcast_fusion
  308.9 0.0 reduce-scatter.5.cloned.1.call-update
  308.9 137.4 %reduce-scatter.5.cloned.1.call-done = f32[8,8,128]{2,1,0:T(8,128)} async-done(((f32[256,8,128]{2,1,0:T(8,128)}), f32[8,8,128]{2,1,0:T(8,128)}) %reduce-scatter.5.cloned.1.call-update) | async-done | bytes 32784 | tf_op jit(solution)/shard_map/reduce_scatter | solution.py:49
  446.3 85.0 %psum.23 = f32[8,8,128]{2,1,0:T(8,128)S(1)} all-reduce(f32[8,8,128]{2,1,0:T(8,128)} %reduce-scatter.5.cloned.1.call-done), channel_id=1, replica_groups=mesh['blk'=16,'bank'=32] {'blk'}, use_global_device_ids=true, to_apply=%region_5.0 | all-reduce | flops 8192 | bytes 65536 | tf_op jit(solution)/shard_map/psum | solution.py:55
  531.3 0.1 divide_convert_fusion
  531.4 0.9 stack.5
  532.3 20.7 %all-to-all-start.1 = ((bf16[32,8,8,128]{3,2,1,0:T(8,128)(2,1)}), bf16[32,8,8,128]{3,2,1,0:T(8,128)(2,1)S(1)}, u32[]{:S(2)}, u32[]{:S(2)}) async-start(bf16[32,8,8,128]{3,2,1,0:T(8,128)(2,1)} %stack.5), calls=%async_computation.3 | async-start | bytes 1048576 | tf_op jit(solution)/shard_map/all_to_all | solution.py:58
  553.0 0.3 copy.14
  553.4 0.7 fusion.56
  554.1 15.5 %all-to-all-done.1 = bf16[32,8,8,128]{3,2,1,0:T(8,128)(2,1)S(1)} async-done(((bf16[32,8,8,128]{3,2,1,0:T(8,128)(2,1)}), bf16[32,8,8,128]{3,2,1,0:T(8,128)(2,1)S(1)}, u32[]{:S(2)}, u32[]{:S(2)}) %all-to-all-start.1) | async-done | bytes 524320 | tf_op jit(solution)/shard_map/all_to_all | solution.py:58
  569.6 1.1 convolution_subtract_fusion
  (1 shorter events, 0.0 us)
Async XLA Ops:
  7.2 172.3 %reduce-scatter.3.cloned.1.call-start = ((), (), s32[]{:S(2)}) async-start(), calls=%async_computation.4 | async-start | bytes 1081344 | tf_op jit(solution)/shard_map/reduce_scatter | solution.py:49
  23.8 1.4 copy-start
  25.4 1.2 copy-start.1
  265.1 37.6 %all-to-all-start = ((bf16[32,8,8,128]{3,2,1,0:T(8,128)(2,1)}), bf16[32,8,8,128]{3,2,1,0:T(8,128)(2,1)S(1)}, u32[]{:S(2)}, u32[]{:S(2)}) async-start(bf16[32,8,8,128]{3,2,1,0:T(8,128)(2,1)} %stack.4), calls=%async_computation.1 | async-start | bytes 1048576 | tf_op jit(solution)/shard_map/all_to_all | solution.py:58
  286.1 160.2 %reduce-scatter.5.cloned.1.call-start = ((), (), s32[]{:S(2)}) async-start(), calls=%async_computation.5 | async-start | bytes 1081344 | tf_op jit(solution)/shard_map/reduce_scatter | solution.py:49
  532.3 37.3 %all-to-all-start.1 = ((bf16[32,8,8,128]{3,2,1,0:T(8,128)(2,1)}), bf16[32,8,8,128]{3,2,1,0:T(8,128)(2,1)S(1)}, u32[]{:S(2)}, u32[]{:S(2)}) async-start(bf16[32,8,8,128]{3,2,1,0:T(8,128)(2,1)} %stack.5), calls=%async_computation.3 | async-start | bytes 1048576 | tf_op jit(solution)/shard_map/all_to_all | solution.py:58
Sparse Core Ops, SparseCore 0:
  28.7 150.6 reduce-scatter.2
  309.0 137.2 reduce-scatter.4

commit v2 on v0

--- a/solution.py
+++ b/solution.py
@@ -52,7 +52,7 @@
             scatter_dimension=0,
             tiled=True,
         )
-        summed = lax.psum(reduced, "blk")
+        summed = jax.lax.all_gather(reduced, axis_name="blk").sum(axis=0)
         center_slice = (summed / counts[None, :, None]).astype(jnp.bfloat16)
         center_all = lax.all_gather(center_slice, "bank", axis=0, tiled=True)
         center_owned = center_slice

time: 616 us -> 531 us (0.86)
  blocking collectives: 390 us -> 304 us
    psum x2 -> x0, blocking collectives: 170 us -> none  [per_device(): summed = lax.psum(reduced, 'blk')]
    all_gather x0 -> x2, blocking collectives: none -> 97.8 us  [per_device(): summed = jax.lax.all_gather(reduced, axis_name='blk').sum(axis=0)]
    all_gather x2, blocking collectives: 111 us -> 97.8 us  [per_device(): center_all = lax.all_gather(center_slice, 'bank', axis=0, tiled=True)]
where the time goes in v2:
time: 531 us; the launch traced here: 530 us
  blocking collectives  304 us (57%)
  waiting for transfers between devices  182 us (34%)
  local copies, waits for them, and re-layouts  14.5 us (3%)
  between operations  14.2 us (3%)
  matrix products  9.63 us (2%)
  other arithmetic  6.67 us (1%)
    reduce_scatter x2, waiting for transfers between devices, per_device(): lax.psum_scatter(jnp.einsum('km,mrl->rkl', member_weights, blocks, precis...  182 us
    psum x1, blocking collectives, per_device(): counts = lax.psum(jnp.sum(onehot, axis=0), ('blk', 'bank'))  108 us
    all_gather x2, blocking collectives, per_device(): center_all = lax.all_gather(center_slice, 'bank', axis=0, tiled=True)  97.8 us
    all_gather x2, blocking collectives, per_device(): summed = jax.lax.all_gather(reduced, axis_name='blk').sum(axis=0)  97.8 us
    convert_element_type x1, local copies, waits for them, and re-layouts, kernel_tables(): kernel_pair = (kernel_line[:, None, :, None] * kernel_line[None, :, None,...  11.3 us
  transfers between devices with their start and end apart: 2, of which 2 were waited for; matrix products, arithmetic and copies ran while one was open for 0% of the time, Pallas kernels for 0%

profile of v2, /device:TPU:1, one launch (start us, length us, event | category | flops | bytes accessed | tf_op | source)
XLA Modules:
  0.0 530.5 jit_solution(10032098381937809484)
XLA Ops:
  7.2 0.0 reduce-scatter.3.cloned.1.call-start
  7.2 5.3 multiply_convert_fusion
  12.5 11.3 %reshape.103 = bf16[1024,1024,1]{1,0,2:T(8,128)(2,1)S(1)} reshape(bf16[32,32,32,32]{3,2,1,0:T(8,128)(2,1)} %multiply_convert_fusion) | data formatting | bytes 4194304 | tf_op jit(solution)/shard_map/convert_element_type | solution.py:18
  23.8 0.0 copy-start
  23.8 0.4 fusion.17
  24.3 0.6 fusion.3
  24.9 0.3 copy.10
  25.2 0.0 copy-done
  25.2 0.2 fusion.5
  25.4 0.0 copy-start.1
  25.5 0.5 fusion.14
  25.9 0.6 fusion.2
  26.5 0.1 reshape_reshape.6
  26.6 0.0 copy-done.1
  26.6 2.0 convolution_bitcast_fusion.2
  28.6 0.0 reduce-scatter.3.cloned.1.call-update
  28.6 0.0 reduce-scatter.5.cloned.1.call-start
  28.7 0.1 convert_reduce_fusion
  28.8 108.1 %psum.7 = f32[8]{0:T(128)S(1)} all-reduce(f32[8]{0:T(128)S(1)} %convert_reduce_fusion), channel_id=1, replica_groups=mesh['blk'=16,'bank'=32] {'blk','bank'}, use_global_device_ids=true, to_apply=%region_3.0 | all-reduce | flops 8 | bytes 64 | tf_op jit(solution)/shard_map/psum | solution.py:40
  136.9 43.4 %reduce-scatter.3.cloned.1.call-done = f32[8,8,128]{2,1,0:T(8,128)} async-done(((f32[256,8,128]{2,1,0:T(8,128)}), f32[8,8,128]{2,1,0:T(8,128)}) %reduce-scatter.3.cloned.1.call-update) | async-done | bytes 32784 | tf_op jit(solution)/shard_map/reduce_scatter | solution.py:49
  180.3 48.8 %all-gather = f32[128,8,128]{2,1,0:T(8,128)S(1)} all-gather(f32[8,8,128]{2,1,0:T(8,128)} %reduce-scatter.3.cloned.1.call-done), channel_id=2, replica_groups=mesh['blk'=16,'bank'=32] {'blk'}, dimensions={0}, use_global_device_ids=true | all-gather | bytes 557056 | tf_op jit(solution)/shard_map/all_gather | solution.py:55
  229.1 0.1 divide_convert_fusion.1
  229.2 49.1 %all_gather.20 = bf16[256,8,128]{2,1,0:T(8,128)(2,1)S(1)} all-gather(bf16[8,8,128]{2,1,0:T(8,128)(2,1)S(1)} %divide_convert_fusion.1), channel_id=1, replica_groups=mesh['blk'=16,'bank'=32] {'bank'}, dimensions={0}, use_global_device_ids=true | all-gather | bytes 540672 | tf_op jit(solution)/shard_map/all_gather | solution.py:57
  278.3 0.3 fusion.37
  278.7 0.8 copy.8
  279.5 1.1 reshape.96
  280.6 0.5 fusion.10
  281.1 0.6 fusion.1
  281.7 0.3 copy.12
  282.1 0.2 fusion.7
  282.3 0.5 fusion.11
  282.8 0.6 convolution_log_fusion
  283.4 0.1 reshape_reshape.7
  283.4 2.0 convolution_bitcast_fusion.1
  285.4 0.0 reduce-scatter.5.cloned.1.call-update
  285.4 0.3 copy.14
  285.8 138.2 %reduce-scatter.5.cloned.1.call-done = f32[8,8,128]{2,1,0:T(8,128)} async-done(((f32[256,8,128]{2,1,0:T(8,128)}), f32[8,8,128]{2,1,0:T(8,128)}) %reduce-scatter.5.cloned.1.call-update) | async-done | bytes 32784 | tf_op jit(solution)/shard_map/reduce_scatter | solution.py:49
  423.9 49.0 %all-gather.1 = f32[128,8,128]{2,1,0:T(8,128)S(1)} all-gather(f32[8,8,128]{2,1,0:T(8,128)} %reduce-scatter.5.cloned.1.call-done), channel_id=3, replica_groups=mesh['blk'=16,'bank'=32] {'blk'}, dimensions={0}, use_global_device_ids=true | all-gather | bytes 557056 | tf_op jit(solution)/shard_map/all_gather | solution.py:55
  473.0 0.1 divide_convert_fusion
  473.1 0.7 fusion.58
  473.8 48.7 %all_gather.23 = bf16[256,8,128]{2,1,0:T(8,128)(2,1)S(1)} all-gather(bf16[8,8,128]{2,1,0:T(8,128)(2,1)S(1)} %divide_convert_fusion), channel_id=1, replica_groups=mesh['blk'=16,'bank'=32] {'bank'}, dimensions={0}, use_global_device_ids=true | all-gather | bytes 540672 | tf_op jit(solution)/shard_map/all_gather | solution.py:57
  522.5 1.1 fusion
  (3 shorter events, 0.1 us)
Async XLA Ops:
  7.2 173.1 %reduce-scatter.3.cloned.1.call-start = ((), (), s32[]{:S(2)}) async-start(), calls=%async_computation.2 | async-start | bytes 1081344 | tf_op jit(solution)/shard_map/reduce_scatter | solution.py:49
  23.8 1.4 copy-start
  25.4 1.2 copy-start.1
  28.6 395.3 %reduce-scatter.5.cloned.1.call-start = ((), (), s32[]{:S(2)}) async-start(), calls=%async_computation.3 | async-start | bytes 1081344 | tf_op jit(solution)/shard_map/reduce_scatter | solution.py:49
Sparse Core Ops, SparseCore 0:
  28.7 151.4 reduce-scatter.2
  285.5 138.3 reduce-scatter.4
